TPU v7x, 128 devices: a whole 4x4x4 slice. The times are simulated.
128 devices in a mesh: gx: 16 (over y, z), gy: 8 (over x, core).
Axes of the slice: x: 4, y: 4, z: 4, core: 2. Of those that a mesh axis runs over, the one named last changes fastest.
Arguments:
- point_feats: bfloat16 [393216, 64], P(('gx', 'gy')), may hold values from -6 to 6
- point_dest: int32 [393216, 1], P(('gx', 'gy')), may hold values from 0 to 127; in each aligned block of 3072 rows (0 to 3071, 3072 to 6143, ...) at most 48 rows name the same one
- point_voxel: int32 [393216], P(('gx', 'gy')), may hold values from 0 to 767
- kernel_map: int32 [27, 98304], P(None, ('gx', 'gy')), may hold values from 0 to 1152, as said below
- border_list: int32 [32, 16, 24], P('gx', 'gy'), may hold values from 0 to 767, as said below
- conv_one: bfloat16 [27, 64, 64], replicated, may hold values from -0.15625 to 0.15625
- conv_two: bfloat16 [27, 64, 64], replicated, may hold values from -0.15625 to 0.15625
- gain_one: float32 [64], replicated, may hold values from 0.25 to 1.75
- gain_two: float32 [64], replicated, may hold values from 0.25 to 1.75
- decoder_in: bfloat16 [64, 128], replicated, may hold values from -0.75 to 0.75
- decoder_bias: float32 [128], replicated, may hold values from -3 to 3
- decoder_out: float32 [128], replicated, may hold values from -0.5 to 0.5
- target: float32 [98304], P(('gx', 'gy')), may hold values from -6 to 6
Outputs:
- sdf_values: float32 [98304], P(('gx', 'gy'))
- loss_value: float32 [], replicated
- grad_conv_one: float32 [27, 64, 64], replicated
- grad_conv_two: float32 [27, 64, 64], replicated
- grad_decoder_in: float32 [64, 128], replicated
- grad_decoder_bias: float32 [128], replicated
- grad_decoder_out: float32 [128], replicated
- grad_points: bfloat16 [393216, 64], P(('gx', 'gy'))
Inputs may be any that keep to these rules, and one draw needn't show every extreme that they name: point_dest names the device gx index * 8 + gy index. Among the rows of one device no device is named by more than 48 rows, and some device is named by exactly 48. `kernel_map`: row k gives each voxel's neighbour at offset k as a row of its device's table: below 768 a local voxel, then 16 * 24 boundary rows, and 1152 the zero row. Offset k is the step (k // 9 - 1, k // 3 % 3 - 1, k % 3 - 1) along the first lateral direction, the second lateral direction and height; row (26) // 2 names the voxel itself. The maps are symmetric: where row k names local voxel u for voxel v, row 26 - k names v for u. Only a voxel listed at slot m of its brick's cell c in border_list names boundary rows, and then only slot m of the cell beside c in the step's lateral direction; the voxel at slot m of that cell names, in row 26 - k, slot m of cell c. A step with no lateral part names only local voxels or the zero row. `border_list`: local voxel rows of the owning device, distinct within a brick; the voxels listed for a brick's cell (2a + i, 2b + j) lie in its rows (2i + j) * 192 to (2i + j + 1) * 192 - 1.
All inputs are finite; a program needn't handle non-finite values.
Results may differ from a plain program's by a relative error of at most 0.011.
Values may be sent and summed in bfloat16 or wider, within the bound.
No kernel may reach another device: no remote copies, remote signals or barrier semaphores. Data moves between devices by JAX's collectives and lax.ppermute only.
A program may use at most 64 MiB of HBM per device.

v0:
```python
import math

import jax
import jax.numpy as jnp
from jax import lax
from jax.sharding import PartitionSpec as P

EPS = 1e-05


def with_halo(array, sides, width):
    for axis, dim in sides:
        peers, length = (lax.axis_size(axis), array.shape[dim])
        up = [(i, (i + 1) % peers) for i in range(peers - 1)]
        down = [(j, i) for i, j in up]
        last = lax.slice_in_dim(array, length - width, length, axis=dim)
        leading = lax.slice_in_dim(array, 0, width, axis=dim)
        before = lax.ppermute(last, axis, up)
        after = lax.ppermute(leading, axis, down)
        array = jnp.concatenate([before, array, after], axis=dim)
    return array


def activate(hidden, gain_vec):
    inverse_rms = lax.rsqrt(jnp.mean(hidden * hidden, axis=-1, keepdims=True) + EPS)
    return jax.nn.silu(hidden * inverse_rms * gain_vec)


def build_table(features, border_list):
    channels = features.shape[1]
    edge_rows = features[border_list]
    neighbour_rows = with_halo(edge_rows, (("gx", 0), ("gy", 1)), 1)
    zero_row = jnp.zeros((1, channels), features.dtype)
    return jnp.concatenate([features, neighbour_rows.reshape(-1, channels), zero_row], axis=0)


def split_blocks(kernel_map):
    offsets, voxels = kernel_map.shape
    block_size = math.gcd(voxels, 256)
    return kernel_map.reshape(offsets, voxels // block_size, block_size).transpose(1, 0, 2)


def select_rows(table, index_rows):
    table_rows = jnp.arange(table.shape[0], dtype=jnp.int32)
    selector = (index_rows[:, :, None] == table_rows[None, None, :]).astype(table.dtype)
    picked = jnp.einsum("knr,rc->knc", selector, table, preferred_element_type=jnp.float32)
    return picked.astype(table.dtype)


def conv_forward(table, kernel_map, weight):
    map_blocks = split_blocks(kernel_map)

    def conv_one_block(index_rows):
        return jnp.einsum(
            "knc,kcd->nd",
            select_rows(table, index_rows),
            weight,
            preferred_element_type=jnp.float32,
        )

    result = lax.map(conv_one_block, map_blocks)
    return result.reshape(-1, weight.shape[2])


def weight_grad_only(table, kernel_map, weight, grad_rows):
    map_blocks = split_blocks(kernel_map)
    grad_blocks = grad_rows.reshape(map_blocks.shape[0], map_blocks.shape[2], grad_rows.shape[1])

    def weight_one_block(running, block_item):
        index_rows, block_grad = block_item
        return (
            running
            + jnp.einsum(
                "knc,nd->kcd",
                select_rows(table, index_rows),
                block_grad,
                preferred_element_type=jnp.float32,
            ),
            None,
        )

    total, _ = lax.scan(
        weight_one_block, jnp.zeros(weight.shape, jnp.float32), (map_blocks, grad_blocks)
    )
    return total


def backward_conv(table, kernel_map, weight, grad_rows, border_list):
    voxels = kernel_map.shape[1]
    channels = grad_rows.shape[1]
    boundary = border_list.shape[2]
    weight_grad = weight_grad_only(table, kernel_map, weight, grad_rows)
    flipped_map = kernel_map[::-1]
    flipped_weight = jnp.swapaxes(weight, 1, 2)
    empty_rows = jnp.zeros((16 * boundary + 1, channels), grad_rows.dtype)
    local_part = conv_forward(
        jnp.concatenate([grad_rows, empty_rows], axis=0), flipped_map, flipped_weight
    )
    border_flat = border_list.reshape(-1)
    border_targets = kernel_map[:, border_flat]
    border_terms = jnp.einsum(
        "bd,kcd->kbc", grad_rows[border_flat], weight, preferred_element_type=jnp.float32
    )
    halo_rows = voxels + jnp.arange(16 * boundary, dtype=jnp.int32)
    selector = (border_targets[:, :, None] == halo_rows[None, None, :]).astype(jnp.float32)
    halo_flat = jnp.einsum("kbr,kbc->rc", selector, border_terms, precision=lax.Precision.HIGHEST)
    halo_grad = halo_flat.reshape(4, 4, boundary, channels)
    rows_end = jnp.stack([halo_grad[0], halo_grad[3]], axis=0)
    cols_end = jnp.stack([halo_grad[:, 0], halo_grad[:, 3]], axis=1)
    corner_end = jnp.stack([rows_end[:, 0], rows_end[:, 3]], axis=1)
    payload = jnp.stack([rows_end[:, 1:3], cols_end[1:3], corner_end], axis=2)
    received = with_halo(payload.astype(jnp.bfloat16), (("gx", 0), ("gy", 1)), 1).astype(
        payload.dtype
    )
    from_rows = jnp.stack([received[0, 1:3, 0], received[3, 1:3, 0]], axis=0)
    from_cols = jnp.stack([received[1:3, 0, 1], received[1:3, 3, 1]], axis=1)
    corner_low = jnp.stack([received[0, 0, 2], received[0, 3, 2]], axis=0)
    corner_high = jnp.stack([received[3, 0, 2], received[3, 3, 2]], axis=0)
    from_corner = jnp.stack([corner_low, corner_high], axis=0)
    folded = halo_grad[1:3, 1:3] + from_rows + from_cols + from_corner
    result = local_part.at[border_list.reshape(-1)].add(folded.reshape(-1, channels))
    return (result, weight_grad)


def send_points(send_feats, send_ids):
    got_feats, got_ids = (
        lax.all_to_all(send_feats, ("gx", "gy"), split_axis=0, concat_axis=0, tiled=True),
        lax.all_to_all(send_ids, ("gx", "gy"), split_axis=0, concat_axis=0, tiled=True),
    )
    return (got_feats, got_ids)


def return_grads(slot_grads):
    returned = lax.all_to_all(slot_grads, ("gx", "gy"), split_axis=0, concat_axis=0, tiled=True)
    return returned


def local(
    point_feats,
    point_dest,
    point_voxel,
    kernel_map,
    border_list,
    conv_one,
    conv_two,
    gain_one,
    gain_two,
    decoder_in,
    decoder_bias,
    decoder_out,
    target,
):
    devices = lax.axis_size("gx") * lax.axis_size("gy")
    voxels = kernel_map.shape[1]
    points, channels = point_feats.shape
    capacity = 2 * points // devices
    destination = point_dest[:, 0]
    order = jnp.argsort(destination, stable=True)
    sorted_dest = destination[order]
    starts = jnp.searchsorted(sorted_dest, jnp.arange(devices, dtype=jnp.int32))
    slot_rank = jnp.arange(points, dtype=jnp.int32) - starts[sorted_dest]
    position = sorted_dest * capacity + slot_rank
    send_feats = (
        jnp.zeros((devices * capacity, channels), point_feats.dtype)
        .at[position]
        .set(point_feats[order])
    )
    send_ids = jnp.full((devices * capacity,), -1, jnp.int32).at[position].set(point_voxel[order])
    got_feats, got_ids = send_points(
        send_feats.reshape(devices, capacity, channels), send_ids.reshape(devices, capacity)
    )
    flat_ids = got_ids.reshape(-1)
    voxel_rows = jnp.arange(voxels, dtype=jnp.int32)
    slot_match = flat_ids[:, None] == voxel_rows[None, :]
    pooled_sum = jnp.einsum(
        "sv,sc->vc",
        slot_match.astype(jnp.bfloat16),
        got_feats.reshape(-1, channels),
        preferred_element_type=jnp.float32,
    )
    counts = jnp.sum(slot_match.astype(jnp.float32), axis=0)
    inverse = 1.0 / jnp.maximum(counts, 1.0)
    x_zero = (pooled_sum * inverse[:, None]).astype(jnp.bfloat16)
    table_one = build_table(x_zero, border_list)
    hidden_one = conv_forward(table_one, kernel_map, conv_one)
    act_one = activate(hidden_one, gain_one).astype(jnp.bfloat16)
    table_two = build_table(act_one, border_list)
    hidden_two = conv_forward(table_two, kernel_map, conv_two)
    block_out = (x_zero.astype(jnp.float32) + activate(hidden_two, gain_two)).astype(jnp.bfloat16)
    pre_dec = jnp.dot(block_out, decoder_in, preferred_element_type=jnp.float32) + decoder_bias
    dec_hidden = jax.nn.silu(pre_dec)
    sdf_values = jnp.sum(dec_hidden * decoder_out, axis=-1)
    whole_count = voxels * devices
    error_sdf = sdf_values - target
    loss_part = jnp.sum(error_sdf * error_sdf) / (2.0 * whole_count)
    grad_sdf = error_sdf / whole_count
    grad_out_part = jnp.sum(dec_hidden * grad_sdf[:, None], axis=0)
    _, pull_silu = jax.vjp(jax.nn.silu, pre_dec)
    grad_pre = pull_silu(grad_sdf[:, None] * decoder_out)[0]
    grad_bias_part = jnp.sum(grad_pre, axis=0)
    grad_pre_low = grad_pre.astype(jnp.bfloat16)
    grad_in_part = lax.dot_general(
        block_out, grad_pre_low, (((0,), (0,)), ((), ())), preferred_element_type=jnp.float32
    )
    grad_block = lax.dot_general(
        grad_pre_low, decoder_in, (((1,), (1,)), ((), ())), preferred_element_type=jnp.float32
    )
    _, pull_two = jax.vjp(lambda hidden: activate(hidden, gain_two), hidden_two)
    grad_hidden_two = pull_two(grad_block)[0].astype(jnp.bfloat16)
    grad_act_one, weight_grad_two = backward_conv(
        table_two, kernel_map, conv_two, grad_hidden_two, border_list
    )
    _, pull_one = jax.vjp(lambda hidden: activate(hidden, gain_one), hidden_one)
    grad_hidden_one = pull_one(grad_act_one)[0].astype(jnp.bfloat16)
    input_part, weight_grad_one = backward_conv(
        table_one, kernel_map, conv_one, grad_hidden_one, border_list
    )
    grad_x_zero = grad_block + input_part
    scaled = grad_x_zero * inverse[:, None]
    slot_values = jnp.einsum(
        "sv,vc->sc", slot_match.astype(jnp.float32), scaled, precision=lax.Precision.HIGHEST
    )
    slot_grads = slot_values.astype(jnp.bfloat16).reshape(devices, capacity, channels)
    returned = return_grads(slot_grads).reshape(-1, channels)
    grad_points = jnp.zeros((points, channels), jnp.bfloat16).at[order].set(returned[position])
    summed = lax.psum(
        (weight_grad_one, weight_grad_two, grad_in_part, grad_bias_part, grad_out_part, loss_part),
        ("gx", "gy"),
    )
    (
        grad_conv_one,
        grad_conv_two,
        grad_decoder_in,
        grad_decoder_bias,
        grad_decoder_out,
        loss_value,
    ) = summed
    return (
        sdf_values,
        loss_value,
        grad_conv_one,
        grad_conv_two,
        grad_decoder_in,
        grad_decoder_bias,
        grad_decoder_out,
        grad_points,
    )


def solution(mesh):
    in_specs = (
        P(("gx", "gy"), None),
        P(("gx", "gy"), None),
        P(("gx", "gy")),
        P(None, ("gx", "gy")),
        P("gx", "gy", None),
        P(),
        P(),
        P(),
        P(),
        P(),
        P(),
        P(),
        P(("gx", "gy")),
    )
    out_specs = (P(("gx", "gy")), P(), P(), P(), P(), P(), P(), P(("gx", "gy"), None))
    return jax.shard_map(local, mesh=mesh, in_specs=in_specs, out_specs=out_specs, check_vma=False)
```

profile of v0, /device:TPU:1, one launch (start us, length us, event | category | flops | bytes accessed | tf_op | source)
XLA Modules:
  0.0 556.9 jit_solution(13134380140512454399)
XLA Ops:
  14.3 17.4 %gather_fusion.1 = s32[3072]{0:T(1024)S(1)} fusion(s32[3072]{0:T(1024)S(1)} %bitcast.265, s32[3072]{0:T(1024)S(1)} %get-tuple-element.565), kind=kCustom, calls=%fused_computation.1 | custom fusion | bytes 36864 | tf_op jit(solution)/shard_map/gather | solution.py:159
  31.7 14.6 %while.90 = (s32[]{:T(128)}, u32[128]{0:T(128)S(1)}, u32[128]{0:T(128)S(1)}, s32[3072]{0:T(1024)S(1)}, s32[]{:T(128)}, /*index=5*/s32[]{:T(128)}, s32[]{}) while((s32[]{:T(128)}, u32[128]{0:T(128)S(1)}, u32[128]{0:T(128)S(1)}, s32[3072]{0:T(1024)S(1)}, s32[]{:T(128)}, /*index=5*/s32[]{:T(128)}, s32[]{}) %tuple.187), condition=%wide.region_2.3_spmd.clone, body=%wide.region_1.2_spmd.clone.sunk | while | flops 2692 | bytes 10348 | solution.py:160
  46.4 18.7 %gather_fusion.2 = s32[3072]{0:T(1024)S(1)} fusion(s32[128]{0:T(128)S(1)} %convert_element_type.73, s32[3072]{0:T(1024)S(1)} %broadcast_clamp_fusion.1), kind=kCustom, calls=%fused_computation.2 | custom fusion | bytes 36864 | tf_op jit(solution)/shard_map/gather | solution.py:161
  65.8 17.4 %gather_fusion.3 = s32[3072]{0:T(1024)S(1)} fusion(s32[3072]{0:T(1024)S(1)} %copy-done.2, s32[3072]{0:T(1024)S(1)} %get-tuple-element.565), kind=kCustom, calls=%fused_computation.3 | custom fusion | bytes 36864 | tf_op jit(solution)/shard_map/gather | solution.py:168
  83.2 11.8 %scatter_custom_fusion = s32[6144]{0:T(1024)S(1)} fusion(s32[3072]{0:T(1024)S(1)} %bitcast.314, s32[3072]{0:T(1024)S(1)} %gather_fusion.3, s32[]{:T(128)} %constant.114.clone.1), kind=kCustom, calls=%fused_computation.205 | custom fusion | bytes 24580 | tf_op jit(solution)/shard_map/scatter | solution.py:168
  95.7 11.5 %all-to-all-start = ((s32[128,1,48]{2,1,0:T(1,128)}), s32[128,1,48]{2,1,0:T(1,128)S(1)}, u32[]{:S(2)}, u32[]{:S(2)}) async-start(s32[128,1,48]{2,1,0:T(1,128)} %bitcast.21), calls=%async_computation | async-start | bytes 131072 | tf_op jit(solution)/shard_map/all_to_all | solution.py:128
  107.6 18.0 %scatter_custom_fusion.1 = bf16[6144,64]{1,0:T(8,128)(2,1)S(1)} fusion(s32[3072]{0:T(1024)S(1)} %bitcast.315, bf16[3072,64]{1,0:T(8,128)(2,1)S(1)} %copy.181, s32[3072]{0:T(1024)S(1)} %get-tuple-element.565, bf16[]{:T(256)} %constant.122.clone.1), kind=kCustom, calls=%fused_computation.105 | custom fusion | bytes 786434 | tf_op jit(solution)/shard_map/scatter | solution.py:166
  127.4 10.3 %all-to-all-start.1 = ((bf16[128,2,1536]{2,1,0:T(2,128)(2,1)}), bf16[128,2,1536]{2,1,0:T(2,128)(2,1)S(1)}, u32[]{:S(2)}, u32[]{:S(2)}) async-start(bf16[128,2,1536]{2,1,0:T(2,128)(2,1)} %reshape.438), calls=%async_computation.1 | async-start | bytes 1572864 | tf_op jit(solution)/shard_map/all_to_all | solution.py:127
  142.2 12.0 %all-to-all-done.1 = bf16[128,2,1536]{2,1,0:T(2,128)(2,1)S(1)} async-done(((bf16[128,2,1536]{2,1,0:T(2,128)(2,1)}), bf16[128,2,1536]{2,1,0:T(2,128)(2,1)S(1)}, u32[]{:S(2)}, u32[]{:S(2)}) %all-to-all-start.1) | async-done | bytes 786464 | tf_op jit(solution)/shard_map/all_to_all | solution.py:127
  174.0 22.4 %while.86 = (s32[]{:T(128)}, f32[3,256,64]{1,2,0:T(8,128)S(1)}, s32[3,27,256]{2,1,0:T(8,128)S(1)}, bf16[1153,64]{0,1:T(8,128)(2,1)}, bf16[27,64,64]{1,2,0:T(8,128)(2,1)S(1)}, /*index=5*/s32[]{:T(128)}) while((s32[]{:T(128)}, f32[3,256,64]{1,2,0:T(8,128)S(1)}, s32[3,27,256]{2,1,0:T(8,128)S(1)}, bf16[1153,64]{0,1:T(8,128)(2,1)}, ...), condition=%wide.region_7.8_spmd, body=%wide.region_6.7_spmd.sunk | while | flops 1085135616 | bytes 743637 | solution.py:61
  212.8 19.7 %while.87 = (s32[]{:T(128)}, f32[3,256,64]{1,2,0:T(8,128)S(1)}, s32[3,27,256]{2,1,0:T(8,128)S(1)}, bf16[1153,64]{0,1:T(8,128)(2,1)S(1)}, bf16[27,64,64]{1,2,0:T(8,128)(2,1)S(1)}, /*index=5*/s32[]{:T(128)}) while((s32[]{:T(128)}, f32[3,256,64]{1,2,0:T(8,128)S(1)}, s32[3,27,256]{2,1,0:T(8,128)S(1)}, bf16[1153,64]{0,1:T(8,128)(2,1)S(1)}, ...), condition=%wide.region_10.11_spmd, body=%wide.region_9.10_spmd.sunk | while | flops 1085135616 | bytes 759893 | solution.py:61
  254.7 19.7 %while.88 = (s32[]{:T(128)}, f32[3,256,64]{1,2,0:T(8,128)S(1)}, s32[3,27,256]{2,1,0:T(8,128)S(1)}, bf16[1153,64]{0,1:T(8,128)(2,1)S(1)}, bf16[27,64,64]{1,2,0:T(8,128)(2,1)S(1)}, /*index=5*/s32[]{:T(128)}) while((s32[]{:T(128)}, f32[3,256,64]{1,2,0:T(8,128)S(1)}, s32[3,27,256]{2,1,0:T(8,128)S(1)}, bf16[1153,64]{0,1:T(8,128)(2,1)S(1)}, ...), condition=%wide.region_17.18_spmd, body=%wide.region_16.17_spmd.sunk | while | flops 1085135616 | bytes 759893 | solution.py:61
  287.7 24.1 %while.92 = (s32[]{:T(128)}, f32[27,64,64]{2,1,0:T(8,128)}, s32[3,27,256]{2,1,0:T(8,128)S(1)}, bf16[1153,64]{0,1:T(8,128)(2,1)S(1)}, bf16[3,256,64]{1,2,0:T(8,128)(2,1)S(1)}, /*index=5*/s32[]{:T(128)}, s32[]{:T(128)}) while((s32[]{:T(128)}, f32[27,64,64]{2,1,0:T(8,128)}, s32[3,27,256]{2,1,0:T(8,128)S(1)}, ...), condition=%wide.region_24.25_spmd.clone, body=%wide.region_23.24_spmd.clone.sunk | while | flops 1085356800 | bytes 1169511 | solution.py:82
  295.0 8.4 %fusion.174 = f32[27,64,64]{2,1,0:T(8,128)} fusion(s32[27,256]{1,0:T(8,128)S(1)} %dynamic-slice_bitcast_fusion.17, f32[27,64,64]{2,1,0:T(8,128)} %get-tuple-element.896, pred[]{:T(512)S(6)} %compare.17, bf16[1153,64]{0,1:T(8,128)(2,1)S(1)} %get-tuple-element.905, bf16[3,256,64]{1,2,0:T(8,128)(2,1)S(1)} %get-tuple-element.906, s32[]{:T(128)S(6)} %copy.316), kind=kOutput, calls=%fused_computation.75.clone.1 | convolution fusion | flops 1085356800 | bytes 1114117 | tf_op jit(solution)/shard_map/while/body/eval_jaxpr/knc,nd->kcd/dot_general | solution.py:73
  303.4 8.4 %fusion.174 = f32[27,64,64]{2,1,0:T(8,128)} fusion(s32[27,256]{1,0:T(8,128)S(1)} %dynamic-slice_bitcast_fusion.17, f32[27,64,64]{2,1,0:T(8,128)} %get-tuple-element.896, pred[]{:T(512)S(6)} %compare.17, bf16[1153,64]{0,1:T(8,128)(2,1)S(1)} %get-tuple-element.905, bf16[3,256,64]{1,2,0:T(8,128)(2,1)S(1)} %get-tuple-element.906, s32[]{:T(128)S(6)} %copy.316), kind=kOutput, calls=%fused_computation.75.clone.1 | convolution fusion | flops 1085356800 | bytes 1114117 | tf_op jit(solution)/shard_map/while/body/eval_jaxpr/knc,nd->kcd/dot_general | solution.py:73
  318.3 22.7 %while.89 = (s32[]{:T(128)}, f32[3,256,64]{1,0,2:T(4,128)S(1)}, s32[3,27,256]{2,1,0:T(8,128)S(1)}, bf16[1153,64]{0,1:T(8,128)(2,1)S(1)}, bf16[27,64,64]{1,2,0:T(8,128)(2,1)S(1)}, /*index=5*/s32[]{:T(128)}, s32[]{:T(128)}) while((s32[]{:T(128)}, f32[3,256,64]{1,0,2:T(4,128)S(1)}, s32[3,27,256]{2,1,0:T(8,128)S(1)}, ...), condition=%wide.region_32.33_spmd, body=%wide.region_31.32_spmd.sunk | while | flops 1085135616 | bytes 779485 | solution.py:61
  344.6 11.2 %fusion.59 = bf16[6144,64]{0,1:T(8,128)(2,1)} fusion(s32[6144]{0:T(1024)S(1)} %copy-done.18, f32[768,64]{0,1:T(8,128)S(1)} %copy.230, f32[768]{0:T(1024)S(1)} %copy-done.31), kind=kOutput, calls=%fused_computation.87 | convolution fusion | flops 3629039616 | bytes 1010688 | tf_op jit(solution)/shard_map/sv,vc->sc/dot_general | solution.py:220
  359.3 11.7 %all-to-all-start.2 = ((bf16[128,2,1536]{2,1,0:T(2,128)(2,1)}), bf16[128,2,1536]{2,1,0:T(2,128)(2,1)S(1)}, u32[]{:S(2)}, u32[]{:S(2)}) async-start(bf16[128,2,1536]{2,1,0:T(2,128)(2,1)} %reshape.440), calls=%async_computation.2 | async-start | bytes 1572864 | tf_op jit(solution)/shard_map/all_to_all | solution.py:134
  371.4 22.5 %while.91 = (s32[]{:T(128)}, f32[27,64,64]{2,1,0:T(8,128)S(1)}, s32[3,27,256]{2,1,0:T(8,128)S(1)}, bf16[1153,64]{0,1:T(8,128)(2,1)}, bf16[3,256,64]{1,2,0:T(8,128)(2,1)}, /*index=5*/s32[]{:T(128)}, s32[]{:T(128)}) while((s32[]{:T(128)}, f32[27,64,64]{2,1,0:T(8,128)S(1)}, s32[3,27,256]{2,1,0:T(8,128)S(1)}, ...), condition=%wide.region_21.22_spmd.clone, body=%wide.region_20.21_spmd.clone.sunk | while | flops 1085356800 | bytes 1164391 | solution.py:82
  378.9 7.5 %fusion.171 = f32[27,64,64]{2,1,0:T(8,128)S(1)} fusion(s32[27,256]{1,0:T(8,128)S(1)} %dynamic-slice_bitcast_fusion.16, f32[27,64,64]{2,1,0:T(8,128)S(1)} %get-tuple-element.875, pred[]{:T(512)S(6)} %compare.16, bf16[1153,64]{0,1:T(8,128)(2,1)} %get-tuple-element.884, bf16[3,256,64]{1,2,0:T(8,128)(2,1)} %get-tuple-element.885, s32[]{:T(128)S(6)} %copy.310), kind=kOutput, calls=%fused_computation.64.clone.1 | convolution fusion | flops 1085356800 | bytes 1108997 | tf_op jit(solution)/shard_map/while/body/eval_jaxpr/knc,nd->kcd/dot_general | solution.py:73
  386.4 7.5 %fusion.171 = f32[27,64,64]{2,1,0:T(8,128)S(1)} fusion(s32[27,256]{1,0:T(8,128)S(1)} %dynamic-slice_bitcast_fusion.16, f32[27,64,64]{2,1,0:T(8,128)S(1)} %get-tuple-element.875, pred[]{:T(512)S(6)} %compare.16, bf16[1153,64]{0,1:T(8,128)(2,1)} %get-tuple-element.884, bf16[3,256,64]{1,2,0:T(8,128)(2,1)} %get-tuple-element.885, s32[]{:T(128)S(6)} %copy.310), kind=kOutput, calls=%fused_computation.64.clone.1 | convolution fusion | flops 1085356800 | bytes 1108997 | tf_op jit(solution)/shard_map/while/body/eval_jaxpr/knc,nd->kcd/dot_general | solution.py:73
  395.8 67.8 %all-reduce.2 = (f32[]{:T(128)}, f32[64,128]{1,0:T(8,128)}, f32[128]{0:T(128)}, f32[128]{0:T(128)}) all-reduce(f32[]{:T(128)S(6)} %div.76, f32[64,128]{1,0:T(8,128)S(1)} %fusion.94, f32[128]{0:T(128)S(1)} %copy-done.34, f32[128]{0:T(128)S(1)} %copy-done.35), channel_id=1, replica_groups=mesh['gx'=16,'gy'=8] {'gx','gy'}, use_global_device_ids=true, to_apply=%region_14.15 | all-reduce | flops 8449 | bytes 67592 | tf_op jit(solution)/shard_map/psum | solution.py:226
  464.6 17.8 %scatter_custom_fusion.4 = bf16[3072,64]{1,0:T(8,128)(2,1)S(1)} fusion(s32[3072]{0:T(1024)} %get-tuple-element.564, bf16[6144,64]{1,0:T(8,128)(2,1)S(1)} %bitcast.278, s32[3072]{0:T(1024)S(1)} %broadcast_clamp_fusion, bf16[]{:T(256)} %constant.122.clone.1), kind=kCustom, calls=%fused_computation.103 | custom fusion | bytes 393728 | tf_op jit(solution)/shard_map/scatter | solution.py:225
  483.3 63.3 %all-reduce.6.cloned.1.call-done = (f32[27,64,64]{2,1,0:T(8,128)}, f32[27,64,64]{2,1,0:T(8,128)}) async-done(((f32[27,64,64]{2,1,0:T(8,128)}, f32[27,64,64]{2,1,0:T(8,128)}), (f32[27,64,64]{2,1,0:T(8,128)}, f32[27,64,64]{2,1,0:T(8,128)})) %all-reduce.6.cloned.1.call-update) | async-done | bytes 884752 | tf_op jit(solution)/shard_map/psum | solution.py:226
  (352 shorter events, 218.7 us)
Async XLA Ops:
  7.2 225.4 %copy-start = (bf16[64,128]{1,0:T(8,128)(2,1)S(1)}, bf16[64,128]{1,0:T(8,128)(2,1)}, u32[]{:S(2)}) copy-start(bf16[64,128]{1,0:T(8,128)(2,1)} %param.36) | copy-start | bytes 49156
  65.8 41.4 %copy-start.10 = (bf16[3072,64]{0,1:T(8,128)(2,1)S(1)}, bf16[3072,64]{0,1:T(8,128)(2,1)}, u32[]{:S(2)}) copy-start(bf16[3072,64]{0,1:T(8,128)(2,1)} %param.27) | copy-start | bytes 1179652
  95.7 31.7 %all-to-all-start = ((s32[128,1,48]{2,1,0:T(1,128)}), s32[128,1,48]{2,1,0:T(1,128)S(1)}, u32[]{:S(2)}, u32[]{:S(2)}) async-start(s32[128,1,48]{2,1,0:T(1,128)} %bitcast.21), calls=%async_computation | async-start | bytes 131072 | tf_op jit(solution)/shard_map/all_to_all | solution.py:128
  127.4 26.8 %all-to-all-start.1 = ((bf16[128,2,1536]{2,1,0:T(2,128)(2,1)}), bf16[128,2,1536]{2,1,0:T(2,128)(2,1)S(1)}, u32[]{:S(2)}, u32[]{:S(2)}) async-start(bf16[128,2,1536]{2,1,0:T(2,128)(2,1)} %reshape.438), calls=%async_computation.1 | async-start | bytes 1572864 | tf_op jit(solution)/shard_map/all_to_all | solution.py:127
  159.1 73.4 %copy-start.8 = (bf16[768,64]{0,1:T(8,128)(2,1)}, bf16[768,64]{0,1:T(8,128)(2,1)S(1)}, u32[]{:S(2)}) copy-start(bf16[768,64]{0,1:T(8,128)(2,1)S(1)} %fusion.69) | copy-start | bytes 294916
  160.0 5.4 collective-permute-start.1
  161.3 4.8 collective-permute-start
  166.1 6.4 %collective-permute-start.3 = (bf16[4,1,24,64]{3,2,1,0:T(8,128)(2,1)S(1)}, bf16[4,1,24,64]{3,2,1,0:T(8,128)(2,1)S(1)}, u32[]{:S(2)}, u32[]{:S(2)}) collective-permute-start(bf16[4,1,24,64]{3,2,1,0:T(8,128)(2,1)S(1)} %get-tuple-element.559), channel_id=1, source_target_pairs={{1,0},{2,1},{3,2},{4,3},{5,4},{6,5},{7,6},{9,8},{10,9},{11,10},{12... | collective-permute-start | bytes 36872 | tf_op jit(solution)/shard_map/ppermute | solution.py:19
  170.0 3.1 collective-permute-start.2
  197.5 5.9 %collective-permute-start.5 = (bf16[1,2,24,64]{3,2,1,0:T(8,128)(2,1)S(1)}, bf16[1,2,24,64]{3,2,1,0:T(8,128)(2,1)S(1)}, u32[]{:S(2)}, u32[]{:S(2)}) collective-permute-start(bf16[1,2,24,64]{3,2,1,0:T(8,128)(2,1)S(1)} %bitcast.321), channel_id=1, source_target_pairs={{8,0},{16,8},{24,16},{32,24},{40,32},{48,40},{56,48},{64,56},{72,6... | collective-permute-start | bytes 18440 | tf_op jit(solution)/shard_map/ppermute | solution.py:19
  198.8 5.4 collective-permute-start.4
  203.4 32.2 %copy-start.22 = (s32[1024]{0:T(1024)}, s32[1024]{0:T(1024)S(1)}, u32[]{:S(2)}) copy-start(s32[1024]{0:T(1024)S(1)} %pad_clamp_fusion.1) | copy-start | bytes 12292
  204.2 8.3 %collective-permute-start.7 = (bf16[4,1,24,64]{3,2,1,0:T(8,128)(2,1)S(1)}, bf16[4,1,24,64]{3,2,1,0:T(8,128)(2,1)S(1)}, u32[]{:S(2)}, u32[]{:S(2)}) collective-permute-start(bf16[4,1,24,64]{3,2,1,0:T(8,128)(2,1)S(1)} %get-tuple-element.557), channel_id=1, source_target_pairs={{1,0},{2,1},{3,2},{4,3},{5,4},{6,5},{7,6},{9,8},{10,9},{11,10},{12... | collective-permute-start | bytes 36872 | tf_op jit(solution)/shard_map/ppermute | solution.py:19
  207.2 5.3 collective-permute-start.6
  239.5 6.7 %collective-permute-start.9 = (bf16[1,2,3,24,64]{4,3,1,0,2:T(8,128)(2,1)}, bf16[1,2,3,24,64]{4,3,1,0,2:T(8,128)(2,1)S(1)}, u32[]{:S(2)}, u32[]{:S(2)}) collective-permute-start(bf16[1,2,3,24,64]{4,3,1,0,2:T(8,128)(2,1)} %get-tuple-element.551), channel_id=1, source_target_pairs={{8,0},{16,8},{24,16},{32,24},{40,32},{48,40},{56,48},{64,56},{72,6... | collective-permute-start | bytes 55304 | tf_op jit(solution)/shard_map/ppermute | solution.py:19
  240.8 5.6 %collective-permute-start.8 = (bf16[1,2,3,24,64]{4,3,1,0,2:T(8,128)(2,1)S(1)}, bf16[1,2,3,24,64]{4,3,1,0,2:T(8,128)(2,1)}, u32[]{:S(2)}, u32[]{:S(2)}) collective-permute-start(bf16[1,2,3,24,64]{4,3,1,0,2:T(8,128)(2,1)S(1)} %get-tuple-element.550), channel_id=1, source_target_pairs={{0,8},{8,16},{16,24},{24,32},{32,40},{40,48},{48,56},{56,64},{64,7... | collective-permute-start | bytes 55304 | tf_op jit(solution)/shard_map/ppermute | solution.py:18
  247.9 26.7 %collective-permute-start.11 = (bf16[4,1,3,24,64]{4,3,1,0,2:T(8,128)(2,1)}, bf16[4,1,3,24,64]{4,3,1,0,2:T(8,128)(2,1)}, u32[]{:S(2)}, u32[]{:S(2)}) collective-permute-start(bf16[4,1,3,24,64]{4,3,1,0,2:T(8,128)(2,1)} %get-tuple-element.539), channel_id=1, source_target_pairs={{1,0},{2,1},{3,2},{4,3},{5,4},{6,5},{7,6},{9,8},{10,9},{11,10},{12... | collective-permute-start | bytes 110600 | tf_op jit(solution)/shard_map/ppermute | solution.py:19
  249.8 24.8 %collective-permute-start.10 = (bf16[4,1,3,24,64]{4,3,1,0,2:T(8,128)(2,1)}, bf16[4,1,3,24,64]{4,3,1,0,2:T(8,128)(2,1)}, u32[]{:S(2)}, u32[]{:S(2)}) collective-permute-start(bf16[4,1,3,24,64]{4,3,1,0,2:T(8,128)(2,1)} %get-tuple-element.538), channel_id=1, source_target_pairs={{0,1},{1,2},{2,3},{3,4},{4,5},{5,6},{6,7},{8,9},{9,10},{10,11},{11... | collective-permute-start | bytes 110600 | tf_op jit(solution)/shard_map/ppermute | solution.py:18
  281.3 30.6 %collective-permute-start.13 = (bf16[1,2,3,24,64]{4,3,1,0,2:T(8,128)(2,1)S(1)}, bf16[1,2,3,24,64]{4,3,1,0,2:T(8,128)(2,1)S(1)}, u32[]{:S(2)}, u32[]{:S(2)}) collective-permute-start(bf16[1,2,3,24,64]{4,3,1,0,2:T(8,128)(2,1)S(1)} %get-tuple-element.549), channel_id=1, source_target_pairs={{8,0},{16,8},{24,16},{32,24},{40,32},{48,40},{56,48},{64,56},{72,6... | collective-permute-start | bytes 55304 | tf_op jit(solution)/shard_map/ppermute | solution.py:19
  282.6 29.3 %collective-permute-start.12 = (bf16[1,2,3,24,64]{4,3,1,0,2:T(8,128)(2,1)S(1)}, bf16[1,2,3,24,64]{4,3,1,0,2:T(8,128)(2,1)S(1)}, u32[]{:S(2)}, u32[]{:S(2)}) collective-permute-start(bf16[1,2,3,24,64]{4,3,1,0,2:T(8,128)(2,1)S(1)} %get-tuple-element.548), channel_id=1, source_target_pairs={{0,8},{8,16},{16,24},{24,32},{32,40},{40,48},{48,56},{56,64},{64,7... | collective-permute-start | bytes 55304 | tf_op jit(solution)/shard_map/ppermute | solution.py:18
  312.6 29.4 %collective-permute-start.15 = (bf16[4,1,3,24,64]{4,3,1,0,2:T(8,128)(2,1)}, bf16[4,1,3,24,64]{4,3,1,0,2:T(8,128)(2,1)}, u32[]{:S(2)}, u32[]{:S(2)}) collective-permute-start(bf16[4,1,3,24,64]{4,3,1,0,2:T(8,128)(2,1)} %get-tuple-element.537), channel_id=1, source_target_pairs={{1,0},{2,1},{3,2},{4,3},{5,4},{6,5},{7,6},{9,8},{10,9},{11,10},{12... | collective-permute-start | bytes 110600 | tf_op jit(solution)/shard_map/ppermute | solution.py:19
  314.5 27.5 %collective-permute-start.14 = (bf16[4,1,3,24,64]{4,3,1,0,2:T(8,128)(2,1)S(1)}, bf16[4,1,3,24,64]{4,3,1,0,2:T(8,128)(2,1)}, u32[]{:S(2)}, u32[]{:S(2)}) collective-permute-start(bf16[4,1,3,24,64]{4,3,1,0,2:T(8,128)(2,1)S(1)} %get-tuple-element.536), channel_id=1, source_target_pairs={{0,1},{1,2},{2,3},{3,4},{4,5},{5,6},{6,7},{8,9},{9,10},{10,11},{11... | collective-permute-start | bytes 110600 | tf_op jit(solution)/shard_map/ppermute | solution.py:18
  359.3 104.2 %all-to-all-start.2 = ((bf16[128,2,1536]{2,1,0:T(2,128)(2,1)}), bf16[128,2,1536]{2,1,0:T(2,128)(2,1)S(1)}, u32[]{:S(2)}, u32[]{:S(2)}) async-start(bf16[128,2,1536]{2,1,0:T(2,128)(2,1)} %reshape.440), calls=%async_computation.2 | async-start | bytes 1572864 | tf_op jit(solution)/shard_map/all_to_all | solution.py:134
  371.1 175.6 %all-reduce.6.cloned.1.call-start = ((), (), s32[]{:S(2)}) async-start(), calls=%async_computation.3 | async-start | bytes 3538944 | tf_op jit(solution)/shard_map/psum | solution.py:226
  (36 other events, 348.1 us)
Sparse Core Ops, SparseCore 0:
  394.9 151.6 all-reduce.5
where the time goes:
time: 565 us; the launch traced here: 557 us
  matrix products  148 us (26%)
  local copies, waits for them, and re-layouts  143 us (25%)
  starting transfers between devices  83.3 us (15%)
  waiting for transfers between devices  77.5 us (14%)
  blocking collectives  67.8 us (12%)
  other arithmetic  20 us (4%)
  between operations  16.5 us (3%)
    dot_general x12, matrix products, conv_one_block(): jnp.einsum('knc,kcd->nd', select_rows(table, index_rows), weight, preferr...  81 us
    psum x1, blocking collectives, local(): lax.psum((weight_grad_one, weight_grad_two, grad_in_part, grad_bias_part,...  67.8 us
    psum x1, waiting for transfers between devices, local(): lax.psum((weight_grad_one, weight_grad_two, grad_in_part, grad_bias_part,...  63.3 us
    dot_general x6, matrix products, weight_one_block(): jnp.einsum('knc,nd->kcd', select_rows(table, index_rows), block_grad, pre...  46.4 us
    ppermute x8, starting transfers between devices, with_halo(): before = lax.ppermute(last, axis, up)  33.7 us
    gather x1, local copies, waits for them, and re-layouts, local(): slot_rank = jnp.arange(points, dtype=jnp.int32) - starts[sorted_dest]  18.7 us
    scatter x1, local copies, waits for them, and re-layouts, local(): send_feats = jnp.zeros((devices * capacity, channels), point_feats.dtype)...  18 us
    scatter x1, local copies, waits for them, and re-layouts, local(): jnp.zeros((points, channels), jnp.bfloat16).at[order]  17.8 us
  transfers between devices with their start and end apart: 20, of which 6 were waited for; matrix products, arithmetic and copies ran while one was open for 24% of the time, Pallas kernels for 0%

commit v1 on v0

--- a/solution.py
+++ b/solution.py
@@ -120,6 +120,38 @@
     folded = halo_grad[1:3, 1:3] + from_rows + from_cols + from_corner
     result = local_part.at[border_list.reshape(-1)].add(folded.reshape(-1, channels))
     return (result, weight_grad)
+
+
+HALVING_STEPS = (("gy", 1), ("gy", 2), ("gx", 1), ("gx", 4), ("gy", 4), ("gx", 2), ("gx", 8))
+
+
+def tree_psum(parts):
+    flat = jnp.concatenate([jnp.ravel(p).astype(jnp.float32) for p in parts])
+    lanes = 128
+    rows = -(-flat.shape[0] // lanes)
+    rows = -(-rows // (8 * 2 ** len(HALVING_STEPS))) * (8 * 2 ** len(HALVING_STEPS))
+    x = jnp.pad(flat, (0, rows * lanes - flat.shape[0])).reshape(rows, lanes)
+    bits = []
+    for axis, mask in HALVING_STEPS:
+        peers = lax.axis_size(axis)
+        bit = (lax.axis_index(axis) // mask) % 2
+        bits.append(bit)
+        half = x.shape[0] // 2
+        low, high = x[:half], x[half:]
+        send = jnp.where(bit == 1, low, high)
+        keep = jnp.where(bit == 1, high, low)
+        x = keep + lax.ppermute(send, axis, [(i, i ^ mask) for i in range(peers)])
+    for (axis, mask), bit in reversed(list(zip(HALVING_STEPS, bits))):
+        peers = lax.axis_size(axis)
+        other = lax.ppermute(x, axis, [(i, i ^ mask) for i in range(peers)])
+        x = jnp.where(bit == 1, jnp.concatenate([other, x]), jnp.concatenate([x, other]))
+    flat = x.reshape(-1)
+    out, start = [], 0
+    for p in parts:
+        size = math.prod(p.shape)
+        out.append(flat[start:start + size].reshape(p.shape))
+        start += size
+    return tuple(out)
 
 
 def send_points(send_feats, send_ids):
@@ -223,10 +255,8 @@
     slot_grads = slot_values.astype(jnp.bfloat16).reshape(devices, capacity, channels)
     returned = return_grads(slot_grads).reshape(-1, channels)
     grad_points = jnp.zeros((points, channels), jnp.bfloat16).at[order].set(returned[position])
-    summed = lax.psum(
-        (weight_grad_one, weight_grad_two, grad_in_part, grad_bias_part, grad_out_part, loss_part),
-        ("gx", "gy"),
-    )
+    parts = (weight_grad_one, weight_grad_two, grad_in_part, grad_bias_part, grad_out_part, loss_part)
+    summed = tree_psum(parts)
     (
         grad_conv_one,
         grad_conv_two,

time: 565 us -> 497 us (0.88)
  blocking collectives: 67.8 us -> 0 us
  starting transfers between devices: 83.3 us -> 107 us
  waiting for transfers between devices: 77.5 us -> 58.2 us
  between operations: 16.5 us -> 3.34 us
  local copies, waits for them, and re-layouts: 143 us -> 151 us
    psum x1 -> x0, blocking collectives: 67.8 us -> none  [local(): lax.psum((weight_grad_one, weight_grad_two, grad_in_part, grad_bias_part,...]
    psum x1 -> x0, waiting for transfers between devices: 63.3 us -> none  [local(): lax.psum((weight_grad_one, weight_grad_two, grad_in_part, grad_bias_part,...]
    ppermute x0 -> x14, starting transfers between devices: none -> 26.5 us  [the longest x7 18.7 us: tree_psum(): x = keep + lax.ppermute(send, axis, [(i, i ^ mask) for i in range(peers)])]
    ppermute x0 -> x14, waiting for transfers between devices: none -> 22.1 us  [the longest x7 11.4 us: tree_psum(): other = lax.ppermute(x, axis, [(i, i ^ mask) for i in range(peers)])]
    all_to_all x1, waiting for transfers between devices: 0.01 us -> 15.3 us  [return_grads(): lax.all_to_all(slot_grads, ('gx', 'gy'), split_axis=0, concat_axis=0, til...]
    ppermute x8, waiting for transfers between devices: 0.02 us -> 7.31 us  [with_halo(): after = lax.ppermute(leading, axis, down)]
    unnamed x90 -> x108, local copies, waits for them, and re-layouts: 12.5 us -> 10.3 us
  transfers between devices with their start and end apart: 20 -> 33, of which waited for: 6 -> 17; matrix products, arithmetic and copies ran while one was open for 24% -> 23% of each run, Pallas kernels for 0% -> 0%
where the time goes in v1:
time: 497 us; the launch traced here: 488 us
  local copies, waits for them, and re-layouts  151 us (30%)
  matrix products  145 us (29%)
  starting transfers between devices  107 us (22%)
  waiting for transfers between devices  58.2 us (12%)
  other arithmetic  22 us (4%)
    dot_general x12, matrix products, conv_one_block(): jnp.einsum('knc,kcd->nd', select_rows(table, index_rows), weight, preferr...  83.8 us
    dot_general x6, matrix products, weight_one_block(): jnp.einsum('knc,nd->kcd', select_rows(table, index_rows), block_grad, pre...  41.9 us
    ppermute x8, starting transfers between devices, with_halo(): before = lax.ppermute(last, axis, up)  29.3 us
    ppermute x7, starting transfers between devices, tree_psum(): x = keep + lax.ppermute(send, axis, [(i, i ^ mask) for i in range(peers)])  18.7 us
    gather x1, local copies, waits for them, and re-layouts, local(): slot_rank = jnp.arange(points, dtype=jnp.int32) - starts[sorted_dest]  18.7 us
    scatter x1, local copies, waits for them, and re-layouts, local(): send_feats = jnp.zeros((devices * capacity, channels), point_feats.dtype)...  18 us
    scatter x1, local copies, waits for them, and re-layouts, local(): jnp.zeros((points, channels), jnp.bfloat16).at[order]  17.8 us
    gather x1, local copies, waits for them, and re-layouts, local(): sorted_dest = destination[order]  17.4 us
  transfers between devices with their start and end apart: 33, of which 17 were waited for; matrix products, arithmetic and copies ran while one was open for 23% of the time, Pallas kernels for 0%

profile of v1, /device:TPU:1, one launch (start us, length us, event | category | flops | bytes accessed | tf_op | source)
XLA Modules:
  0.0 488.0 jit_solution(11984630714418117048)
XLA Ops:
  7.8 17.4 %gather_fusion.1 = s32[3072]{0:T(1024)S(1)} fusion(s32[3072]{0:T(1024)S(1)} %bitcast.285, s32[3072]{0:T(1024)S(1)} %get-tuple-element.563), kind=kCustom, calls=%fused_computation.1 | custom fusion | bytes 36864 | tf_op jit(solution)/shard_map/gather | solution.py:191
  25.2 14.6 %while.90 = (s32[]{:T(128)}, u32[128]{0:T(128)S(1)}, u32[128]{0:T(128)S(1)}, s32[3072]{0:T(1024)S(1)}, s32[]{:T(128)}, /*index=5*/s32[]{:T(128)}, s32[]{}) while((s32[]{:T(128)}, u32[128]{0:T(128)S(1)}, u32[128]{0:T(128)S(1)}, s32[3072]{0:T(1024)S(1)}, s32[]{:T(128)}, /*index=5*/s32[]{:T(128)}, s32[]{}) %tuple.189), condition=%wide.region_2.3_spmd.clone, body=%wide.region_1.2_spmd.clone.sunk | while | flops 2692 | bytes 10340 | solution.py:192
  39.8 18.7 %gather_fusion.2 = s32[3072]{0:T(1024)S(1)} fusion(s32[128]{0:T(128)S(1)} %convert_element_type.75, s32[3072]{0:T(1024)S(1)} %broadcast_clamp_fusion.1), kind=kCustom, calls=%fused_computation.2 | custom fusion | bytes 36864 | tf_op jit(solution)/shard_map/gather | solution.py:193
  59.2 17.4 %gather_fusion.3 = s32[3072]{0:T(1024)S(1)} fusion(s32[3072]{0:T(1024)S(1)} %copy-done.2, s32[3072]{0:T(1024)S(1)} %get-tuple-element.563), kind=kCustom, calls=%fused_computation.3 | custom fusion | bytes 36864 | tf_op jit(solution)/shard_map/gather | solution.py:200
  76.6 11.8 %scatter_custom_fusion = s32[6144]{0:T(1024)S(1)} fusion(s32[3072]{0:T(1024)S(1)} %bitcast.334, s32[3072]{0:T(1024)S(1)} %gather_fusion.3, s32[]{:T(128)} %constant.213.clone.1), kind=kCustom, calls=%fused_computation.228 | custom fusion | bytes 24580 | tf_op jit(solution)/shard_map/scatter | solution.py:200
  89.2 11.5 %all-to-all-start = ((s32[128,1,48]{2,1,0:T(1,128)}), s32[128,1,48]{2,1,0:T(1,128)S(1)}, u32[]{:S(2)}, u32[]{:S(2)}) async-start(s32[128,1,48]{2,1,0:T(1,128)} %bitcast.21), calls=%async_computation | async-start | bytes 131072 | tf_op jit(solution)/shard_map/all_to_all | solution.py:160
  101.1 18.0 %scatter_custom_fusion.1 = bf16[6144,64]{1,0:T(8,128)(2,1)S(1)} fusion(s32[3072]{0:T(1024)S(1)} %bitcast.335, bf16[3072,64]{1,0:T(8,128)(2,1)S(1)} %copy.181, s32[3072]{0:T(1024)S(1)} %get-tuple-element.563, bf16[]{:T(256)} %constant.221.clone.1), kind=kCustom, calls=%fused_computation.109 | custom fusion | bytes 786434 | tf_op jit(solution)/shard_map/scatter | solution.py:198
  120.8 10.0 %all-to-all-start.1 = ((bf16[128,2,1536]{2,1,0:T(2,128)(2,1)}), bf16[128,2,1536]{2,1,0:T(2,128)(2,1)S(1)}, u32[]{:S(2)}, u32[]{:S(2)}) async-start(bf16[128,2,1536]{2,1,0:T(2,128)(2,1)} %reshape.496), calls=%async_computation.1 | async-start | bytes 1572864 | tf_op jit(solution)/shard_map/all_to_all | solution.py:159
  135.4 12.0 %all-to-all-done.1 = bf16[128,2,1536]{2,1,0:T(2,128)(2,1)S(1)} async-done(((bf16[128,2,1536]{2,1,0:T(2,128)(2,1)}), bf16[128,2,1536]{2,1,0:T(2,128)(2,1)S(1)}, u32[]{:S(2)}, u32[]{:S(2)}) %all-to-all-start.1) | async-done | bytes 786464 | tf_op jit(solution)/shard_map/all_to_all | solution.py:159
  168.7 19.7 %while.86 = (s32[]{:T(128)}, f32[3,256,64]{1,2,0:T(8,128)S(1)}, s32[3,27,256]{2,1,0:T(8,128)S(1)}, bf16[1153,64]{0,1:T(8,128)(2,1)S(1)}, bf16[27,64,64]{1,2,0:T(8,128)(2,1)S(1)}, /*index=5*/s32[]{:T(128)}) while((s32[]{:T(128)}, f32[3,256,64]{1,2,0:T(8,128)S(1)}, s32[3,27,256]{2,1,0:T(8,128)S(1)}, bf16[1153,64]{0,1:T(8,128)(2,1)S(1)}, ...), condition=%wide.region_7.8_spmd, body=%wide.region_6.7_spmd.sunk | while | flops 1085135616 | bytes 759893 | solution.py:61
  207.3 22.4 %while.87 = (s32[]{:T(128)}, f32[3,256,64]{1,2,0:T(8,128)S(1)}, s32[3,27,256]{2,1,0:T(8,128)S(1)}, bf16[1153,64]{0,1:T(8,128)(2,1)}, bf16[27,64,64]{1,2,0:T(8,128)(2,1)S(1)}, /*index=5*/s32[]{:T(128)}) while((s32[]{:T(128)}, f32[3,256,64]{1,2,0:T(8,128)S(1)}, s32[3,27,256]{2,1,0:T(8,128)S(1)}, bf16[1153,64]{0,1:T(8,128)(2,1)}, ...), condition=%wide.region_10.11_spmd, body=%wide.region_9.10_spmd.sunk | while | flops 1085135616 | bytes 743637 | solution.py:61
  207.4 7.4 %fusion.164 = f32[3,256,64]{1,2,0:T(8,128)S(1)} fusion(f32[3,256,64]{1,2,0:T(8,128)S(1)} %get-tuple-element.836, s32[]{:T(128)S(6)} %copy.298, bf16[27,64,64]{1,2,0:T(8,128)(2,1)S(1)} %get-tuple-element.845, s32[27,256]{1,0:T(8,128)S(1)} %dynamic-slice_bitcast_fusion.13, bf16[1153,64]{0,1:T(8,128)(2,1)} %get-tuple-element.844), kind=kOutput, calls=%fused_computation.32.clone.1 | convolution fusion | flops 1085135616 | bytes 688260 | tf_op jit(solution)/shard_map/while/body/eval_jaxpr/knc,kcd->nd/dot_general | solution.py:54
  242.3 22.5 %while.92 = (s32[]{:T(128)}, f32[27,64,64]{2,1,0:T(8,128)S(1)}, s32[3,27,256]{2,1,0:T(8,128)S(1)}, bf16[1153,64]{0,1:T(8,128)(2,1)}, bf16[3,256,64]{1,2,0:T(8,128)(2,1)S(1)}, /*index=5*/s32[]{:T(128)}, s32[]{:T(128)}) while((s32[]{:T(128)}, f32[27,64,64]{2,1,0:T(8,128)S(1)}, s32[3,27,256]{2,1,0:T(8,128)S(1)}, ...), condition=%wide.region_21.22_spmd.clone, body=%wide.region_20.21_spmd.clone.sunk | while | flops 1085356800 | bytes 1595623 | solution.py:82
  242.4 7.4 %fusion.177 = f32[27,64,64]{2,1,0:T(8,128)S(1)} fusion(s32[27,256]{1,0:T(8,128)S(1)} %dynamic-slice_bitcast_fusion.17, f32[27,64,64]{2,1,0:T(8,128)S(1)} %get-tuple-element.894, pred[]{:T(512)S(6)} %compare.37, bf16[1153,64]{0,1:T(8,128)(2,1)} %get-tuple-element.903, bf16[3,256,64]{1,2,0:T(8,128)(2,1)S(1)} %get-tuple-element.904, s32[]{:T(128)S(6)} %copy.317), kind=kOutput, calls=%fused_computation.75.clone.1 | convolution fusion | flops 1085356800 | bytes 1540229 | tf_op jit(solution)/shard_map/while/body/eval_jaxpr/knc,nd->kcd/dot_general | solution.py:73
  249.8 7.5 %fusion.177 = f32[27,64,64]{2,1,0:T(8,128)S(1)} fusion(s32[27,256]{1,0:T(8,128)S(1)} %dynamic-slice_bitcast_fusion.17, f32[27,64,64]{2,1,0:T(8,128)S(1)} %get-tuple-element.894, pred[]{:T(512)S(6)} %compare.37, bf16[1153,64]{0,1:T(8,128)(2,1)} %get-tuple-element.903, bf16[3,256,64]{1,2,0:T(8,128)(2,1)S(1)} %get-tuple-element.904, s32[]{:T(128)S(6)} %copy.317), kind=kOutput, calls=%fused_computation.75.clone.1 | convolution fusion | flops 1085356800 | bytes 1540229 | tf_op jit(solution)/shard_map/while/body/eval_jaxpr/knc,nd->kcd/dot_general | solution.py:73
  257.3 7.5 %fusion.177 = f32[27,64,64]{2,1,0:T(8,128)S(1)} fusion(s32[27,256]{1,0:T(8,128)S(1)} %dynamic-slice_bitcast_fusion.17, f32[27,64,64]{2,1,0:T(8,128)S(1)} %get-tuple-element.894, pred[]{:T(512)S(6)} %compare.37, bf16[1153,64]{0,1:T(8,128)(2,1)} %get-tuple-element.903, bf16[3,256,64]{1,2,0:T(8,128)(2,1)S(1)} %get-tuple-element.904, s32[]{:T(128)S(6)} %copy.317), kind=kOutput, calls=%fused_computation.75.clone.1 | convolution fusion | flops 1085356800 | bytes 1540229 | tf_op jit(solution)/shard_map/while/body/eval_jaxpr/knc,nd->kcd/dot_general | solution.py:73
  271.6 22.4 %while.88 = (s32[]{:T(128)}, f32[3,256,64]{1,2,0:T(8,128)S(1)}, s32[3,27,256]{2,1,0:T(8,128)S(1)}, bf16[1153,64]{0,1:T(8,128)(2,1)}, bf16[27,64,64]{1,2,0:T(8,128)(2,1)S(1)}, /*index=5*/s32[]{:T(128)}) while((s32[]{:T(128)}, f32[3,256,64]{1,2,0:T(8,128)S(1)}, s32[3,27,256]{2,1,0:T(8,128)S(1)}, bf16[1153,64]{0,1:T(8,128)(2,1)}, ...), condition=%wide.region_15.16_spmd, body=%wide.region_14.15_spmd.sunk | while | flops 1085135616 | bytes 743637 | solution.py:61
  303.1 19.7 %while.91 = (s32[]{:T(128)}, f32[27,64,64]{2,1,0:T(8,128)S(1)}, s32[3,27,256]{2,1,0:T(8,128)S(1)}, bf16[1153,64]{0,1:T(8,128)(2,1)S(1)}, bf16[3,256,64]{1,2,0:T(8,128)(2,1)S(1)}, /*index=5*/s32[]{:T(128)}, s32[]{:T(128)}) while((s32[]{:T(128)}, f32[27,64,64]{2,1,0:T(8,128)S(1)}, s32[3,27,256]{2,1,0:T(8,128)S(1)}, ...), condition=%wide.region_19.20_spmd.clone, body=%wide.region_18.19_spmd.clone.sunk | while | flops 1085356800 | bytes 1611879 | solution.py:82
  323.3 27.3 %while.89 = (s32[]{:T(128)}, f32[3,256,64]{1,0,2:T(4,128)}, s32[3,27,256]{2,1,0:T(8,128)S(1)}, bf16[1153,64]{0,1:T(8,128)(2,1)S(1)}, bf16[27,64,64]{1,2,0:T(8,128)(2,1)S(1)}, /*index=5*/s32[]{:T(128)}, s32[]{:T(128)}) while((s32[]{:T(128)}, f32[3,256,64]{1,0,2:T(4,128)}, s32[3,27,256]{2,1,0:T(8,128)S(1)}, bf16[1153,64]{0,1:T(8,128)(2,1)S(1)}, ...), condition=%wide.region_26.27_spmd, body=%wide.region_25.26_spmd.sunk | while | flops 1085135616 | bytes 779485 | solution.py:61
  367.6 10.3 %collective-permute-start.15 = (f32[128,128]{1,0:T(8,128)S(1)}, f32[128,128]{1,0:T(8,128)S(1)}, u32[]{:S(2)}, u32[]{:S(2)}) collective-permute-start(f32[128,128]{1,0:T(8,128)S(1)} %slice_select_fusion.2), channel_id=1, source_target_pairs={{0,32},{8,40},{16,48},{24,56},{32,0},{40,8},{48,16},{56,24},{64,96... | collective-permute-start | bytes 196616 | tf_op jit(solution)/shard_map/ppermute | solution.py:143
  417.0 10.6 %fusion.59 = bf16[6144,64]{0,1:T(8,128)(2,1)S(1)} fusion(s32[6144]{0:T(1024)S(1)} %copy-done.24, f32[768,64]{0,1:T(8,128)S(1)} %copy.230, f32[768]{0:T(1024)S(1)} %copy-done.39), kind=kOutput, calls=%fused_computation.87 | convolution fusion | flops 3629039616 | bytes 1010688 | tf_op jit(solution)/shard_map/sv,vc->sc/dot_general | solution.py:252
  430.2 16.0 %all-to-all-start.2 = ((bf16[128,2,1536]{2,1,0:T(2,128)(2,1)}), bf16[128,2,1536]{2,1,0:T(2,128)(2,1)S(1)}, u32[]{:S(2)}, u32[]{:S(2)}) async-start(bf16[128,2,1536]{2,1,0:T(2,128)(2,1)} %reshape.498), calls=%async_computation.2 | async-start | bytes 1572864 | tf_op jit(solution)/shard_map/all_to_all | solution.py:166
  447.4 15.3 %all-to-all-done.2 = bf16[128,2,1536]{2,1,0:T(2,128)(2,1)S(1)} async-done(((bf16[128,2,1536]{2,1,0:T(2,128)(2,1)}), bf16[128,2,1536]{2,1,0:T(2,128)(2,1)S(1)}, u32[]{:S(2)}, u32[]{:S(2)}) %all-to-all-start.2) | async-done | bytes 786464 | tf_op jit(solution)/shard_map/all_to_all | solution.py:166
  463.8 17.8 %scatter_custom_fusion.4 = bf16[3072,64]{1,0:T(8,128)(2,1)S(1)} fusion(s32[3072]{0:T(1024)} %get-tuple-element.562, bf16[6144,64]{1,0:T(8,128)(2,1)S(1)} %bitcast.299, s32[3072]{0:T(1024)S(1)} %broadcast_clamp_fusion, bf16[]{:T(256)} %constant.221.clone.1), kind=kCustom, calls=%fused_computation.107 | custom fusion | bytes 393728 | tf_op jit(solution)/shard_map/scatter | solution.py:257
  (426 shorter events, 266.8 us)
Async XLA Ops:
  89.2 31.7 %all-to-all-start = ((s32[128,1,48]{2,1,0:T(1,128)}), s32[128,1,48]{2,1,0:T(1,128)S(1)}, u32[]{:S(2)}, u32[]{:S(2)}) async-start(s32[128,1,48]{2,1,0:T(1,128)} %bitcast.21), calls=%async_computation | async-start | bytes 131072 | tf_op jit(solution)/shard_map/all_to_all | solution.py:160
  120.8 26.5 %all-to-all-start.1 = ((bf16[128,2,1536]{2,1,0:T(2,128)(2,1)}), bf16[128,2,1536]{2,1,0:T(2,128)(2,1)S(1)}, u32[]{:S(2)}, u32[]{:S(2)}) async-start(bf16[128,2,1536]{2,1,0:T(2,128)(2,1)} %reshape.496), calls=%async_computation.1 | async-start | bytes 1572864 | tf_op jit(solution)/shard_map/all_to_all | solution.py:159
  153.2 5.4 %collective-permute-start.1 = (bf16[1,2,24,64]{3,2,1,0:T(8,128)(2,1)S(1)}, bf16[1,2,24,64]{3,2,1,0:T(8,128)(2,1)S(1)}, u32[]{:S(2)}, u32[]{:S(2)}) collective-permute-start(bf16[1,2,24,64]{3,2,1,0:T(8,128)(2,1)S(1)} %bitcast.340), channel_id=1, source_target_pairs={{8,0},{16,8},{24,16},{32,24},{40,32},{48,40},{56,48},{64,56},{72,6... | collective-permute-start | bytes 18440 | tf_op jit(solution)/shard_map/ppermute | solution.py:19
  159.3 6.4 %collective-permute-start.2 = (bf16[4,1,24,64]{3,2,1,0:T(8,128)(2,1)S(1)}, bf16[4,1,24,64]{3,2,1,0:T(8,128)(2,1)S(1)}, u32[]{:S(2)}, u32[]{:S(2)}) collective-permute-start(bf16[4,1,24,64]{3,2,1,0:T(8,128)(2,1)S(1)} %get-tuple-element.556), channel_id=1, source_target_pairs={{0,1},{1,2},{2,3},{3,4},{4,5},{5,6},{6,7},{8,9},{9,10},{10,11},{11... | collective-permute-start | bytes 36872 | tf_op jit(solution)/shard_map/ppermute | solution.py:18
  163.4 5.1 %collective-permute-start.3 = (bf16[4,1,24,64]{3,2,1,0:T(8,128)(2,1)S(1)}, bf16[4,1,24,64]{3,2,1,0:T(8,128)(2,1)S(1)}, u32[]{:S(2)}, u32[]{:S(2)}) collective-permute-start(bf16[4,1,24,64]{3,2,1,0:T(8,128)(2,1)S(1)} %get-tuple-element.557), channel_id=1, source_target_pairs={{1,0},{2,1},{3,2},{4,3},{5,4},{6,5},{7,6},{9,8},{10,9},{11,10},{12... | collective-permute-start | bytes 36872 | tf_op jit(solution)/shard_map/ppermute | solution.py:19
  190.2 5.9 %collective-permute-start.5 = (bf16[1,2,24,64]{3,2,1,0:T(8,128)(2,1)S(1)}, bf16[1,2,24,64]{3,2,1,0:T(8,128)(2,1)S(1)}, u32[]{:S(2)}, u32[]{:S(2)}) collective-permute-start(bf16[1,2,24,64]{3,2,1,0:T(8,128)(2,1)S(1)} %bitcast.341), channel_id=1, source_target_pairs={{8,0},{16,8},{24,16},{32,24},{40,32},{48,40},{56,48},{64,56},{72,6... | collective-permute-start | bytes 18440 | tf_op jit(solution)/shard_map/ppermute | solution.py:19
  191.5 5.4 %collective-permute-start.4 = (bf16[1,2,24,64]{3,2,1,0:T(8,128)(2,1)S(1)}, bf16[1,2,24,64]{3,2,1,0:T(8,128)(2,1)S(1)}, u32[]{:S(2)}, u32[]{:S(2)}) collective-permute-start(bf16[1,2,24,64]{3,2,1,0:T(8,128)(2,1)S(1)} %bitcast.339), channel_id=1, source_target_pairs={{0,8},{8,16},{16,24},{24,32},{32,40},{40,48},{48,56},{56,64},{64,7... | collective-permute-start | bytes 18440 | tf_op jit(solution)/shard_map/ppermute | solution.py:18
  197.5 7.6 %collective-permute-start.6 = (bf16[4,1,24,64]{3,2,1,0:T(8,128)(2,1)}, bf16[4,1,24,64]{3,2,1,0:T(8,128)(2,1)S(1)}, u32[]{:S(2)}, u32[]{:S(2)}) collective-permute-start(bf16[4,1,24,64]{3,2,1,0:T(8,128)(2,1)} %get-tuple-element.554), channel_id=1, source_target_pairs={{0,1},{1,2},{2,3},{3,4},{4,5},{5,6},{6,7},{8,9},{9,10},{10,11},{11... | collective-permute-start | bytes 36872 | tf_op jit(solution)/shard_map/ppermute | solution.py:18
  200.2 5.5 %collective-permute-start.7 = (bf16[4,1,24,64]{3,2,1,0:T(8,128)(2,1)}, bf16[4,1,24,64]{3,2,1,0:T(8,128)(2,1)}, u32[]{:S(2)}, u32[]{:S(2)}) collective-permute-start(bf16[4,1,24,64]{3,2,1,0:T(8,128)(2,1)} %get-tuple-element.555), channel_id=1, source_target_pairs={{1,0},{2,1},{3,2},{4,3},{5,4},{6,5},{7,6},{9,8},{10,9},{11,10},{12... | collective-permute-start | bytes 36872 | tf_op jit(solution)/shard_map/ppermute | solution.py:19
  236.7 28.8 %collective-permute-start.8 = (bf16[1,2,3,24,64]{4,3,1,0,2:T(8,128)(2,1)}, bf16[1,2,3,24,64]{4,3,1,0,2:T(8,128)(2,1)S(1)}, u32[]{:S(2)}, u32[]{:S(2)}) collective-permute-start(bf16[1,2,3,24,64]{4,3,1,0,2:T(8,128)(2,1)} %get-tuple-element.548), channel_id=1, source_target_pairs={{0,8},{8,16},{16,24},{24,32},{32,40},{40,48},{48,56},{56,64},{64,7... | collective-permute-start | bytes 55304 | tf_op jit(solution)/shard_map/ppermute | solution.py:18
  240.6 24.9 %collective-permute-start.9 = (bf16[1,2,3,24,64]{4,3,1,0,2:T(8,128)(2,1)S(1)}, bf16[1,2,3,24,64]{4,3,1,0,2:T(8,128)(2,1)S(1)}, u32[]{:S(2)}, u32[]{:S(2)}) collective-permute-start(bf16[1,2,3,24,64]{4,3,1,0,2:T(8,128)(2,1)S(1)} %get-tuple-element.549), channel_id=1, source_target_pairs={{8,0},{16,8},{24,16},{32,24},{40,32},{48,40},{56,48},{64,56},{72,6... | collective-permute-start | bytes 55304 | tf_op jit(solution)/shard_map/ppermute | solution.py:19
  266.2 29.9 %collective-permute-start.10 = (bf16[4,1,3,24,64]{4,3,1,0,2:T(8,128)(2,1)}, bf16[4,1,3,24,64]{4,3,1,0,2:T(8,128)(2,1)}, u32[]{:S(2)}, u32[]{:S(2)}) collective-permute-start(bf16[4,1,3,24,64]{4,3,1,0,2:T(8,128)(2,1)} %get-tuple-element.536), channel_id=1, source_target_pairs={{0,1},{1,2},{2,3},{3,4},{4,5},{5,6},{6,7},{8,9},{9,10},{10,11},{11... | collective-permute-start | bytes 110600 | tf_op jit(solution)/shard_map/ppermute | solution.py:18
  269.5 26.6 %collective-permute-start.11 = (bf16[4,1,3,24,64]{4,3,1,0,2:T(8,128)(2,1)}, bf16[4,1,3,24,64]{4,3,1,0,2:T(8,128)(2,1)}, u32[]{:S(2)}, u32[]{:S(2)}) collective-permute-start(bf16[4,1,3,24,64]{4,3,1,0,2:T(8,128)(2,1)} %get-tuple-element.537), channel_id=1, source_target_pairs={{1,0},{2,1},{3,2},{4,3},{5,4},{6,5},{7,6},{9,8},{10,9},{11,10},{12... | collective-permute-start | bytes 110600 | tf_op jit(solution)/shard_map/ppermute | solution.py:19
  353.9 7.9 %collective-permute-start.13 = (f32[512,128]{1,0:T(8,128)S(1)}, f32[512,128]{1,0:T(8,128)S(1)}, u32[]{:S(2)}, u32[]{:S(2)}) collective-permute-start(f32[512,128]{1,0:T(8,128)S(1)} %slice_select_fusion), channel_id=1, source_target_pairs={{0,2},{1,3},{2,0},{3,1},{4,6},{5,7},{6,4},{7,5},{8,10},{9,11},{10,... | collective-permute-start | bytes 786440 | tf_op jit(solution)/shard_map/ppermute | solution.py:143
  361.9 5.7 %collective-permute-start.14 = (f32[256,128]{1,0:T(8,128)S(1)}, f32[256,128]{1,0:T(8,128)S(1)}, u32[]{:S(2)}, u32[]{:S(2)}) collective-permute-start(f32[256,128]{1,0:T(8,128)S(1)} %slice_select_fusion.1), channel_id=1, source_target_pairs={{0,8},{8,0},{16,24},{24,16},{32,40},{40,32},{48,56},{56,48},{64,72... | collective-permute-start | bytes 393224 | tf_op jit(solution)/shard_map/ppermute | solution.py:143
  364.4 13.6 %collective-permute-start.26 = (bf16[1,2,3,24,64]{4,3,1,0,2:T(8,128)(2,1)S(1)}, bf16[1,2,3,24,64]{4,3,1,0,2:T(8,128)(2,1)S(1)}, u32[]{:S(2)}, u32[]{:S(2)}) collective-permute-start(bf16[1,2,3,24,64]{4,3,1,0,2:T(8,128)(2,1)S(1)} %get-tuple-element.546), channel_id=1, source_target_pairs={{0,8},{8,16},{16,24},{24,32},{32,40},{40,48},{48,56},{56,64},{64,7... | collective-permute-start | bytes 55304 | tf_op jit(solution)/shard_map/ppermute | solution.py:18
  366.3 11.7 %collective-permute-start.27 = (bf16[1,2,3,24,64]{4,3,1,0,2:T(8,128)(2,1)S(1)}, bf16[1,2,3,24,64]{4,3,1,0,2:T(8,128)(2,1)S(1)}, u32[]{:S(2)}, u32[]{:S(2)}) collective-permute-start(bf16[1,2,3,24,64]{4,3,1,0,2:T(8,128)(2,1)S(1)} %get-tuple-element.547), channel_id=1, source_target_pairs={{8,0},{16,8},{24,16},{32,24},{40,32},{48,40},{56,48},{64,56},{72,6... | collective-permute-start | bytes 55304 | tf_op jit(solution)/shard_map/ppermute | solution.py:19
  367.6 12.2 %collective-permute-start.15 = (f32[128,128]{1,0:T(8,128)S(1)}, f32[128,128]{1,0:T(8,128)S(1)}, u32[]{:S(2)}, u32[]{:S(2)}) collective-permute-start(f32[128,128]{1,0:T(8,128)S(1)} %slice_select_fusion.2), channel_id=1, source_target_pairs={{0,32},{8,40},{16,48},{24,56},{32,0},{40,8},{48,16},{56,24},{64,96... | collective-permute-start | bytes 196616 | tf_op jit(solution)/shard_map/ppermute | solution.py:143
  379.8 8.8 %collective-permute-start.16 = (f32[64,128]{1,0:T(8,128)S(1)}, f32[64,128]{1,0:T(8,128)S(1)}, u32[]{:S(2)}, u32[]{:S(2)}) collective-permute-start(f32[64,128]{1,0:T(8,128)S(1)} %slice_select_fusion.3), channel_id=1, source_target_pairs={{0,4},{1,5},{2,6},{3,7},{4,0},{5,1},{6,2},{7,3},{8,12},{9,13},{10,... | collective-permute-start | bytes 98312 | tf_op jit(solution)/shard_map/ppermute | solution.py:143
  381.9 6.9 %collective-permute-start.28 = (bf16[4,1,3,24,64]{4,3,1,0,2:T(8,128)(2,1)S(1)}, bf16[4,1,3,24,64]{4,3,1,0,2:T(8,128)(2,1)S(1)}, u32[]{:S(2)}, u32[]{:S(2)}) collective-permute-start(bf16[4,1,3,24,64]{4,3,1,0,2:T(8,128)(2,1)S(1)} %get-tuple-element.534), channel_id=1, source_target_pairs={{0,1},{1,2},{2,3},{3,4},{4,5},{5,6},{6,7},{8,9},{9,10},{10,11},{11... | collective-permute-start | bytes 110600 | tf_op jit(solution)/shard_map/ppermute | solution.py:18
  386.7 5.9 %collective-permute-start.29 = (bf16[4,1,3,24,64]{4,3,1,0,2:T(8,128)(2,1)S(1)}, bf16[4,1,3,24,64]{4,3,1,0,2:T(8,128)(2,1)S(1)}, u32[]{:S(2)}, u32[]{:S(2)}) collective-permute-start(bf16[4,1,3,24,64]{4,3,1,0,2:T(8,128)(2,1)S(1)} %get-tuple-element.535), channel_id=1, source_target_pairs={{1,0},{2,1},{3,2},{4,3},{5,4},{6,5},{7,6},{9,8},{10,9},{11,10},{12... | collective-permute-start | bytes 110600 | tf_op jit(solution)/shard_map/ppermute | solution.py:19
  416.9 29.4 %collective-permute-start.24 = (f32[512,128]{1,0:T(8,128)S(1)}, f32[512,128]{1,0:T(8,128)S(1)}, u32[]{:S(2)}, u32[]{:S(2)}) collective-permute-start(f32[512,128]{1,0:T(8,128)S(1)} %maximum_select_fusion.2), channel_id=1, source_target_pairs={{0,2},{1,3},{2,0},{3,1},{4,6},{5,7},{6,4},{7,5},{8,10},{9,11},{10,... | collective-permute-start | bytes 786440 | tf_op jit(solution)/shard_map/ppermute | solution.py:146
  430.2 32.6 %all-to-all-start.2 = ((bf16[128,2,1536]{2,1,0:T(2,128)(2,1)}), bf16[128,2,1536]{2,1,0:T(2,128)(2,1)S(1)}, u32[]{:S(2)}, u32[]{:S(2)}) async-start(bf16[128,2,1536]{2,1,0:T(2,128)(2,1)} %reshape.498), calls=%async_computation.2 | async-start | bytes 1572864 | tf_op jit(solution)/shard_map/all_to_all | solution.py:166
  446.3 36.3 %collective-permute-start.25 = (f32[1024,128]{1,0:T(8,128)S(1)}, f32[1024,128]{1,0:T(8,128)}, u32[]{:S(2)}, u32[]{:S(2)}) collective-permute-start(f32[1024,128]{1,0:T(8,128)S(1)} %maximum_select_fusion.1), channel_id=1, source_target_pairs={{0,1},{1,0},{2,3},{3,2},{4,5},{5,4},{6,7},{7,6},{8,9},{9,8},{10,11... | collective-permute-start | bytes 1572872 | tf_op jit(solution)/shard_map/ppermute | solution.py:146
  (57 other events, 839.3 us)
